TPU v7x, 32 devices: a whole 2x2x4 slice. The times are simulated.
32 devices in a mesh: dp: 8 (over z, x), fsdp: 4 (over y, core).
Axes of the slice: x: 2, y: 2, z: 4, core: 2. Of those that a mesh axis runs over, the one named last changes fastest.
Arguments:
- dec_hidden: bfloat16 [1024, 4096], P('dp'), may hold values from -18 to 18
- w_query: bfloat16 [4096, 2048], P(None, 'fsdp'), may hold values from -0.01171875 to 0.01171875
- enc_states: bfloat16 [2, 1536, 2048], P(None, 'dp', 'fsdp')
- w_out: bfloat16 [2048, 4096], P('fsdp'), may hold values from -0.5 to 0.5
- norm_gain: float32 [4096], replicated, may hold values from 0.25 to 1.75
- w_vocab: bfloat16 [4096, 16384], P(None, 'fsdp'), may hold values from -1 to 1
- enc_segment: int32 [1536], replicated, may hold values from 0 to 3, as said below
- dec_segment: int32 [1024], P('dp'), may hold values from 0 to 3, as said below
- seg_map: int32 [8, 4], replicated, may hold values from 0 to 31, as said below
- targets: int32 [1024], P('dp'), may hold values from 0 to 16383
- loss_mask: int32 [1024], P('dp'), may hold values from 0 to 1, as said below
Outputs:
- mean_loss: float32 [], replicated
- grad_hidden: bfloat16 [1024, 4096], P('dp', 'fsdp')
- grad_gain: float32 [4096], P('fsdp')
Inputs may be any that keep to these rules, and one draw needn't show every extreme that they name: `enc_segment`: each encoder row of 192 tokens holds 4 segments numbered in order, never falling, each nonempty and at most 80 tokens long; one segment of every row is exactly 80 long. `dec_segment`: each decoder row of 128 tokens holds 4 segments numbered in order, never falling, each nonempty and at most 56 tokens long; one segment of every row is exactly 56 long. seg_map[b, j] names the encoder segment (encoder row times 4 plus its number in that row) read by segment j of decoder row b. Every encoder segment is named exactly once. The encoder row read in column j is (b + o_j) mod 8, with offsets o_j that are the same for every decoder row and differ between columns; one of them is 4 and one is 7. The segments of one encoder row go to different decoder rows. `loss_mask`: the first token of every decoder row has mask 1.
All inputs are finite; a program needn't handle non-finite values.
Results may differ from a plain program's by a relative error of at most 0.0086.
Values may be sent and summed in bfloat16 or wider, within the bound.
No kernel may reach another device: no remote copies, remote signals or barrier semaphores. Data moves between devices by JAX's collectives and lax.ppermute only.
A program may use at most 128 MiB of HBM per device.

v0:
```python
import jax
import jax.numpy as jnp
from jax import lax
from jax.sharding import PartitionSpec as P

HEAD_DIM = 64


def joined(x, axis, combine):
    everything = jax.tree.map(lambda part: lax.all_gather(part, axis), x)
    leading = jax.tree.map(lambda part: part[0], everything)

    def turn(k, so_far):
        return combine(so_far, jax.tree.map(lambda part: part[k], everything))

    return lax.fori_loop(1, lax.axis_size(axis), turn, leading)


def merge_totals(first_set, second_set):
    larger = jnp.maximum(first_set[0], second_set[0])
    combined = first_set[1] * jnp.exp(first_set[0] - larger) + second_set[1] * jnp.exp(
        second_set[0] - larger
    )
    return (larger, combined, first_set[2] + second_set[2])


def attend(carry, block, block_ids, queries, sources):
    run_max, run_sum, run_acc = carry
    block_rows = block.shape[1]
    heads_here = queries.shape[1]
    keys_block = block[0].astype(jnp.float32).reshape(block_rows, heads_here, HEAD_DIM)
    values_block = block[1].astype(jnp.float32).reshape(block_rows, heads_here, HEAD_DIM)
    scores = jnp.einsum("ihd,jhd->hij", queries, keys_block)
    allowed = (sources[:, None] == block_ids[None, :])[None]
    new_max = jnp.maximum(run_max, jnp.max(jnp.where(allowed, scores, jnp.float32(-1e30)), 2))
    weights = jnp.where(allowed, jnp.exp(scores - new_max[:, :, None]), 0.0)
    run_sum = jnp.sum(weights, 2)
    run_acc = jnp.einsum("hij,jhd->hid", weights, values_block)
    return (new_max, run_sum, run_acc)


def body(
    dec_hidden,
    w_query,
    enc_states,
    w_out,
    norm_gain,
    w_vocab,
    enc_segment,
    dec_segment,
    seg_map,
    targets,
    loss_mask,
):
    dp_index = lax.axis_index("dp")
    fsdp_index = lax.axis_index("fsdp")
    dp_count = lax.axis_size("dp")
    dec_len, width = dec_hidden.shape
    enc_len = enc_states.shape[1]
    heads_here = w_query.shape[1] // HEAD_DIM
    segments = seg_map.shape[1]
    feature_count = width // lax.axis_size("fsdp")
    vocab_here = w_vocab.shape[1]
    map_row = lax.dynamic_index_in_dim(seg_map, dp_index, 0, keepdims=False)
    segment_picks = dec_segment[:, None] == jnp.arange(segments)[None, :]
    sources = jnp.sum(jnp.where(segment_picks, map_row[None, :], 0), 1)
    query_proj = jnp.dot(dec_hidden, w_query, preferred_element_type=jnp.float32).astype(
        jnp.bfloat16
    )
    queries = (
        lax.optimization_barrier(query_proj)
        .astype(jnp.float32)
        .reshape(dec_len, heads_here, HEAD_DIM)
    )
    start_state = (
        jnp.full((heads_here, dec_len), -1e30, jnp.float32),
        jnp.zeros((heads_here, dec_len), jnp.float32),
        jnp.zeros((heads_here, dec_len, HEAD_DIM), jnp.float32),
    )
    global_ids = jnp.arange(dp_count * enc_len) // enc_len * segments + enc_segment
    state = attend(
        start_state,
        lax.all_gather(enc_states, "dp", axis=1, tiled=True),
        global_ids,
        queries,
        sources,
    )
    run_max, run_sum, run_acc = state
    attended = (
        (run_acc / run_sum[:, :, None])
        .transpose(1, 0, 2)
        .reshape(dec_len, heads_here * HEAD_DIM)
        .astype(jnp.bfloat16)
    )
    feature_start = fsdp_index * feature_count
    gain_part = lax.dynamic_slice_in_dim(norm_gain, feature_start, feature_count, 0)
    summed_full = lax.psum(
        jnp.dot(attended, w_out, preferred_element_type=jnp.float32), "fsdp"
    ) + dec_hidden.astype(jnp.float32)
    inv_root = lax.rsqrt(jnp.sum(summed_full * summed_full, 1) / width + 1e-06)
    unit_full = summed_full * inv_root[:, None]
    normed_full = (unit_full * norm_gain).astype(jnp.bfloat16)
    logits = jnp.dot(normed_full, w_vocab, preferred_element_type=jnp.float32)
    unit_part = lax.dynamic_slice_in_dim(unit_full, feature_start, feature_count, 1)
    local_target = targets - fsdp_index * vocab_here
    picked = jnp.arange(vocab_here)[None, :] == local_target[:, None]
    local_top = jnp.max(logits, 1)
    local_total = jnp.sum(jnp.exp(logits - local_top[:, None]), 1)
    local_pick = jnp.sum(jnp.where(picked, logits, 0.0), 1)
    row_top, row_total, target_logit = joined(
        (local_top, local_total, local_pick), "fsdp", merge_totals
    )
    log_total = row_top + jnp.log(row_total)
    mask_float = loss_mask.astype(jnp.float32)
    grad_logits = (
        mask_float[:, None] * (jnp.exp(logits - log_total[:, None]) - picked.astype(jnp.float32))
    ).astype(jnp.bfloat16)
    grad_normed = lax.psum_scatter(
        lax.dot_general(
            w_vocab, grad_logits, (((1,), (1,)), ((), ())), preferred_element_type=jnp.float32
        ),
        "fsdp",
        scatter_dimension=0,
        tiled=True,
    ).T
    grad_unit = grad_normed * gain_part
    inner_total = lax.psum(jnp.sum(grad_unit * unit_part, 1), "fsdp")
    grad_summed = inv_root[:, None] * (grad_unit - unit_part * (inner_total / width)[:, None])
    gain_local = jnp.sum(grad_normed * unit_part, 0)
    token_count, loss_total, gain_total = lax.psum(
        (jnp.sum(mask_float), jnp.sum(mask_float * (log_total - target_logit)), gain_local), "dp"
    )
    return (
        loss_total / token_count,
        (grad_summed / token_count).astype(jnp.bfloat16),
        gain_total / token_count,
    )


def solution(mesh):
    in_specs = (
        P("dp", None),
        P(None, "fsdp"),
        P(None, "dp", "fsdp"),
        P("fsdp", None),
        P(),
        P(None, "fsdp"),
        P(),
        P("dp"),
        P(),
        P("dp"),
        P("dp"),
    )
    out_specs = (P(), P("dp", "fsdp"), P("fsdp"))
    return jax.shard_map(body, mesh=mesh, in_specs=in_specs, out_specs=out_specs, check_vma=False)
```

profile of v0, /device:TPU:0, one launch (start us, length us, event | category | flops | bytes accessed | tf_op | source)
XLA Modules:
  0.0 266.7 jit_solution(12701368455562883856)
XLA Ops:
  7.2 0.7 all-gather.8.cloned.1.call-update
  8.0 3.2 %convolution_convert_fusion = bf16[128,512]{1,0:T(8,128)(2,1)S(1)} fusion(bf16[128,4096]{1,0:T(8,128)(2,1)} %param.13, bf16[4096,512]{1,0:T(8,128)(2,1)} %param.14), kind=kOutput, calls=%fused_computation.27 | convolution fusion | flops 536936448 | bytes 5373952 | tf_op jit(solution)/shard_map/dot_general | solution.py:67
  11.4 0.2 dynamic-slice_reduce_fusion
  11.7 0.2 broadcast_compare_fusion
  11.8 61.6 %all-gather.8.cloned.1.call-done = bf16[2,1536,512]{2,1,0:T(8,128)(2,1)} async-done(((bf16[2,192,512]{2,1,0:T(8,128)(2,1)}), bf16[2,1536,512]{2,1,0:T(8,128)(2,1)}) %all-gather.8.cloned.1.call-update) | async-done | bytes 3145744 | tf_op jit(solution)/shard_map/all_gather | solution.py:83
  73.4 3.2 %fusion.29 = (bf16[1,1536,512]{2,1,0:T(8,128)(2,1)}, bf16[1,1536,512]{2,1,0:T(8,128)(2,1)S(1)}) fusion(bf16[2,1536,512]{2,1,0:T(8,128)(2,1)} %all-gather.8.cloned.1.call-done), kind=kLoop, calls=%fused_computation.65 | loop fusion | bytes 6291456 | tf_op jit(solution)/shard_map/slice | solution.py:31
  76.6 1.7 copy.24
  78.3 3.8 %select_reduce_fusion = (f32[8,128]{1,0:T(8,128)S(1)}, f32[8,128,1536]{2,1,0:T(8,128)}) fusion(pred[128,1536]{1,0:T(8,128)(4,1)S(1)} %broadcast_compare_fusion, bf16[128,8,64]{0,2,1:T(8,128)(2,1)S(1)} %bitcast.64, bf16[1536,8,64]{0,2,1:T(8,128)(2,1)S(1)} %bitcast.62), kind=kOutput, calls=%fused_computation.11 | convolution fusion | flops 204471296 | bytes 8196096 | tf_op jit(solution)/shard_map/ihd,jhd->hij/dot_general | solution.py:33
  82.1 0.7 copy.25
  82.9 4.3 %fusion.7 = f32[8,128]{1,0:T(8,128)S(1)} fusion(f32[8,128,1536]{2,1,0:T(8,128)} %get-tuple-element.214, f32[8,128]{1,0:T(8,128)S(1)} %broadcast_maximum_fusion, pred[128,1536]{1,0:T(8,128)(4,1)S(1)} %broadcast_compare_fusion), kind=kLoop, calls=%fused_computation.12 | loop fusion | flops 4717568 | bytes 6496256 | tf_op jit(solution)/shard_map/reduce_sum | solution.py:37
  87.1 0.3 copy-done.2
  87.5 1.4 fusion.15
  88.8 0.8 copy-done.7
  89.6 2.0 fusion.31
  91.8 0.6 copy-done.10
  92.3 49.5 %all-reduce.3.cloned.1.call-done = f32[128,4096]{1,0:T(8,128)} async-done(((f32[128,4096]{1,0:T(8,128)}), f32[128,4096]{1,0:T(8,128)}) %all-reduce.3.cloned.1.call-update) | async-done | bytes 2097168 | tf_op jit(solution)/shard_map/psum | solution.py:97
  141.9 2.1 multiply_reduce_fusion
  144.1 0.4 fusion.12
  144.5 0.3 copy-done.8
  144.8 13.7 %fusion.30 = (f32[128]{0:T(128)S(1)}, f32[128,4096]{1,0:T(8,128)S(1)}) fusion(bf16[4096,4096]{1,0:T(8,128)(2,1)} %param.18, f32[128,4096]{1,0:T(8,128)S(1)} %fusion.12, f32[4096]{0:T(1024)S(1)} %copy-done.8), kind=kOutput, calls=%fused_computation.66 | convolution fusion | flops 4296540160 | bytes 37765632 | tf_op jit(solution)/shard_map/dot_general | solution.py:103
  158.6 0.7 select_reduce_fusion.1
  159.3 5.0 %all-gather.5 = f32[4,1,128]{2,1,0:T(1,128)S(1)} all-gather(f32[1,1,128]{2,1,0:T(1,128)S(1)} %bitcast.72), channel_id=4, replica_groups=mesh['dp'=8,'fsdp'=4] {'fsdp'}, dimensions={0}, use_global_device_ids=true | all-gather | bytes 2560 | tf_op jit(solution)/shard_map/all_gather | solution.py:10
  164.3 5.0 %all-gather.4 = f32[4,1,128]{2,1,0:T(1,128)S(1)} all-gather(f32[1,1,128]{2,1,0:T(1,128)S(1)} %bitcast.71), channel_id=3, replica_groups=mesh['dp'=8,'fsdp'=4] {'fsdp'}, dimensions={0}, use_global_device_ids=true | all-gather | bytes 2560 | tf_op jit(solution)/shard_map/all_gather | solution.py:10
  169.3 5.2 %all-gather.3 = f32[4,1,128]{2,1,0:T(1,128)S(1)} all-gather(f32[1,1,128]{2,1,0:T(1,128)S(1)} %bitcast.69), channel_id=2, replica_groups=mesh['dp'=8,'fsdp'=4] {'fsdp'}, dimensions={0}, use_global_device_ids=true | all-gather | bytes 2560 | tf_op jit(solution)/shard_map/all_gather | solution.py:10
  174.7 0.6 convert_reduce_fusion
  175.3 17.3 %convolution_bitcast_fusion = f32[4096,128]{0,1:T(8,128)} fusion(bf16[4096,4096]{1,0:T(8,128)(2,1)} %param.18, f32[128,4096]{1,0:T(8,128)S(1)} %get-tuple-element.216, f32[128]{0:T(128)S(1)} %get-tuple-element.209, f32[128]{0:T(128)S(1)} %convert_element_type.30, s32[128]{0:T(128)S(1)} %broadcast_subtract_fusion), kind=kOutput, calls=%fused_computation.14 | convolution fusion | flops 4298113024 | bytes 37750272 | tf_op jit(solution)/shard_map/dot_general | solution.py:119
  192.6 31.7 %reduce-scatter.2.cloned.1.call-done = f32[1024,128]{0,1:T(8,128)} async-done(((f32[4096,128]{0,1:T(8,128)}), f32[1024,128]{0,1:T(8,128)}) %reduce-scatter.2.cloned.1.call-update) | async-done | bytes 524304 | tf_op jit(solution)/shard_map/reduce_scatter | solution.py:118
  224.3 1.2 fusion.21
  225.5 5.8 %psum.38 = f32[128]{0:T(128)S(1)} all-reduce(f32[128]{0:T(128)S(1)} %get-tuple-element.185), channel_id=1, replica_groups=mesh['dp'=8,'fsdp'=4] {'fsdp'}, use_global_device_ids=true, to_apply=%region_16.17 | all-reduce | flops 128 | bytes 1024 | tf_op jit(solution)/shard_map/psum | solution.py:127
  231.2 22.5 %all-reduce = (f32[]{:T(128)}, f32[]{:T(128)}, f32[1024]{0:T(1024)S(1)}) all-reduce(f32[]{:T(128)} %get-tuple-element.189, f32[]{:T(128)} %get-tuple-element.188, f32[1024]{0:T(1024)S(1)} %get-tuple-element.184), channel_id=1, replica_groups=mesh['dp'=8,'fsdp'=4] {'dp'}, use_global_device_ids=true, to_apply=%region_11.12 | all-reduce | flops 1026 | bytes 8208 | tf_op jit(solution)/shard_map/psum | solution.py:130
  253.8 1.3 broadcast_divide_fusion
  256.4 2.6 divide_convert_fusion
  (43 shorter events, 0.7 us)
Async XLA Ops:
  7.2 4.2 %copy-start = (s32[8,4]{0,1:T(4,128)S(1)}, s32[8,4]{0,1:T(4,128)}, u32[]{:S(2)}) copy-start(s32[8,4]{0,1:T(4,128)} %param.21) | copy-start | bytes 388
  7.2 66.2 %all-gather.8.cloned.1.call-start = ((), (), s32[]{:S(2)}) async-start(), calls=%async_computation.1 | async-start | bytes 3538944 | tf_op jit(solution)/shard_map/all_gather | solution.py:83
  7.9 133.9 %all-reduce.3.cloned.1.call-start = ((), (), s32[]{:S(2)}) async-start(), calls=%async_computation.2 | async-start | bytes 4194304 | tf_op jit(solution)/shard_map/psum | solution.py:97
  8.0 3.6 %copy-start.11 = (s32[128]{0:T(128)S(1)}, s32[128]{0:T(128)}, u32[]{:S(2)}) copy-start(s32[128]{0:T(128)} %param.20) | copy-start | bytes 1540
  8.0 3.7 %copy-start.9 = (s32[1536]{0:T(1024)S(1)}, s32[1536]{0:T(1024)}, u32[]{:S(2)}) copy-start(s32[1536]{0:T(1024)} %param.19) | copy-start | bytes 18436
  82.8 4.6 %copy-start.2 = (f32[8,128,1536]{2,1,0:T(8,128)S(1)}, f32[8,128,1536]{2,1,0:T(8,128)}, u32[]{:S(2)}) copy-start(f32[8,128,1536]{2,1,0:T(8,128)} %get-tuple-element.214) | copy-start | bytes 18874372
  87.4 2.2 copy-start.7
  91.7 0.7 copy-start.10
  91.7 0.7 copy-start.12
  91.7 50.2 %copy-start.5 = (bf16[128,4096]{1,0:T(8,128)(2,1)S(1)}, bf16[128,4096]{1,0:T(8,128)(2,1)}, u32[]{:S(2)}) copy-start(bf16[128,4096]{1,0:T(8,128)(2,1)} %param.13) | copy-start | bytes 3145732
  91.7 132.6 %reduce-scatter.2.cloned.1.call-start = ((), (), s32[]{:S(2)}) async-start(), calls=%async_computation.3 | async-start | bytes 2621440 | tf_op jit(solution)/shard_map/reduce_scatter | solution.py:118
  141.9 2.2 copy-start.6
  144.1 0.7 copy-start.8
  144.8 13.8 %copy-start.3 = (f32[128,4096]{1,0:T(8,128)}, f32[128,4096]{1,0:T(8,128)S(1)}, u32[]{:S(2)}) copy-start(f32[128,4096]{1,0:T(8,128)S(1)} %fusion.12) | copy-start | bytes 6291460
  192.6 31.7 %copy-start.4 = (f32[128,4096]{1,0:T(8,128)S(1)}, f32[128,4096]{1,0:T(8,128)}, u32[]{:S(2)}) copy-start(f32[128,4096]{1,0:T(8,128)} %copy-done.3) | copy-start | bytes 6291460
  192.6 66.5 %copy-start.1 = (s32[8,4]{0,1:T(4,128)S(1)}, s32[8,4]{0,1:T(4,128)}, u32[]{:S(2)}) copy-start(s32[8,4]{0,1:T(4,128)} %param.21) | copy-start | bytes 388
Sparse Core Ops, SparseCore 0:
  10.2 63.1 all-gather.7
  91.8 49.9 all-reduce.2
  192.7 31.5 reduce-scatter.1
where the time goes:
time: 267 us
  waiting for transfers between devices  143 us (54%)
  blocking collectives  43.5 us (16%)
  matrix products  41.5 us (16%)
  between operations  16.4 us (6%)
  other arithmetic  13.6 us (5%)
  local copies, waits for them, and re-layouts  8.11 us (3%)
    all_gather x1, waiting for transfers between devices, body(): lax.all_gather(enc_states, 'dp', axis=1, tiled=True)  61.6 us
    psum x1, waiting for transfers between devices, body(): lax.psum(jnp.dot(attended, w_out, preferred_element_type=jnp.float32), 'f...  49.5 us
    reduce_scatter x1, waiting for transfers between devices, body(): lax.psum_scatter(lax.dot_general(w_vocab, grad_logits, (((1,), (1,)), (()...  31.7 us
    psum x1, blocking collectives, body(): lax.psum((jnp.sum(mask_float), jnp.sum(mask_float * (log_total - target_l...  22.5 us
    dot_general x1, matrix products, body(): lax.dot_general(w_vocab, grad_logits, (((1,), (1,)), ((), ())), preferred...  17.3 us
    all_gather x3, blocking collectives, joined(): everything = jax.tree.map(lambda part: lax.all_gather(part, axis), x)  15.3 us
    dot_general x1, matrix products, body(): logits = jnp.dot(normed_full, w_vocab, preferred_element_type=jnp.float32)  13.7 us
    psum x1, blocking collectives, body(): inner_total = lax.psum(jnp.sum(grad_unit * unit_part, 1), 'fsdp')  5.75 us
  transfers between devices with their start and end apart: 3, of which 3 were waited for; matrix products, arithmetic and copies ran while one was open for 1% of the time, Pallas kernels for 0%

commit v1 on v0

--- a/solution.py
+++ b/solution.py
@@ -94,8 +94,8 @@
     )
     feature_start = fsdp_index * feature_count
     gain_part = lax.dynamic_slice_in_dim(norm_gain, feature_start, feature_count, 0)
-    summed_full = lax.psum(
-        jnp.dot(attended, w_out, preferred_element_type=jnp.float32), "fsdp"
+    summed_full = jnp.sum(
+        lax.all_gather(jnp.dot(attended, w_out, preferred_element_type=jnp.float32), "fsdp"), axis=0
     ) + dec_hidden.astype(jnp.float32)
     inv_root = lax.rsqrt(jnp.sum(summed_full * summed_full, 1) / width + 1e-06)
     unit_full = summed_full * inv_root[:, None]

time: 267 us -> 277 us (1.037)
  waiting for transfers between devices: 143 us -> 150 us
    all_gather x0 -> x1, waiting for transfers between devices: none -> 56.4 us  [body(): lax.all_gather(jnp.dot(attended, w_out, preferred_element_type=jnp.float3...]
    psum x1 -> x0, waiting for transfers between devices: 49.5 us -> none  [body(): lax.psum(jnp.dot(attended, w_out, preferred_element_type=jnp.float32), 'f...]
    reduce_sum x0 -> x1, other arithmetic: none -> 4.32 us  [body(): jnp.sum(lax.all_gather(jnp.dot(attended, w_out, preferred_element_type=jn...]
where the time goes in v1:
time: 277 us; the launch traced here: 276 us
  waiting for transfers between devices  150 us (54%)
  blocking collectives  43.5 us (16%)
  matrix products  41.6 us (15%)
  between operations  16.4 us (6%)
  other arithmetic  16.1 us (6%)
  local copies, waits for them, and re-layouts  8.08 us (3%)
    all_gather x1, waiting for transfers between devices, body(): lax.all_gather(enc_states, 'dp', axis=1, tiled=True)  61.6 us
    all_gather x1, waiting for transfers between devices, body(): lax.all_gather(jnp.dot(attended, w_out, preferred_element_type=jnp.float3...  56.4 us
    reduce_scatter x1, waiting for transfers between devices, body(): lax.psum_scatter(lax.dot_general(w_vocab, grad_logits, (((1,), (1,)), (()...  31.6 us
    psum x1, blocking collectives, body(): lax.psum((jnp.sum(mask_float), jnp.sum(mask_float * (log_total - target_l...  22.5 us
    dot_general x1, matrix products, body(): lax.dot_general(w_vocab, grad_logits, (((1,), (1,)), ((), ())), preferred...  17.3 us
    all_gather x3, blocking collectives, joined(): everything = jax.tree.map(lambda part: lax.all_gather(part, axis), x)  15.3 us
    dot_general x1, matrix products, body(): logits = jnp.dot(normed_full, w_vocab, preferred_element_type=jnp.float32)  13.7 us
    psum x1, blocking collectives, body(): inner_total = lax.psum(jnp.sum(grad_unit * unit_part, 1), 'fsdp')  5.75 us
  transfers between devices with their start and end apart: 3, of which 3 were waited for; matrix products, arithmetic and copies ran while one was open for 1% of the time, Pallas kernels for 0%

profile of v1, /device:TPU:0, one launch (start us, length us, event | category | flops | bytes accessed | tf_op | source)
XLA Modules:
  0.0 276.1 jit_solution(6576611071541854144)
XLA Ops:
  7.2 0.7 all-gather.10.cloned.1.call-update
  8.0 3.2 %convolution_convert_fusion = bf16[128,512]{1,0:T(8,128)(2,1)S(1)} fusion(bf16[128,4096]{1,0:T(8,128)(2,1)} %param.13, bf16[4096,512]{1,0:T(8,128)(2,1)} %param.14), kind=kOutput, calls=%fused_computation.27 | convolution fusion | flops 536936448 | bytes 5373952 | tf_op jit(solution)/shard_map/dot_general | solution.py:67
  11.4 0.2 dynamic-slice_reduce_fusion
  11.8 61.6 %all-gather.10.cloned.1.call-done = bf16[2,1536,512]{2,1,0:T(8,128)(2,1)} async-done(((bf16[2,192,512]{2,1,0:T(8,128)(2,1)}), bf16[2,1536,512]{2,1,0:T(8,128)(2,1)}) %all-gather.10.cloned.1.call-update) | async-done | bytes 3145744 | tf_op jit(solution)/shard_map/all_gather | solution.py:83
  73.4 3.2 %fusion.29 = (bf16[1,1536,512]{2,1,0:T(8,128)(2,1)}, bf16[1,1536,512]{2,1,0:T(8,128)(2,1)S(1)}) fusion(bf16[2,1536,512]{2,1,0:T(8,128)(2,1)} %all-gather.10.cloned.1.call-done), kind=kLoop, calls=%fused_computation.65 | loop fusion | bytes 6291456 | tf_op jit(solution)/shard_map/slice | solution.py:31
  76.6 1.7 copy.24
  78.3 3.8 %select_reduce_fusion = (f32[8,128]{1,0:T(8,128)S(1)}, f32[8,128,1536]{2,1,0:T(8,128)}) fusion(pred[128,1536]{1,0:T(8,128)(4,1)S(1)} %broadcast_compare_fusion, bf16[128,8,64]{0,2,1:T(8,128)(2,1)S(1)} %bitcast.66, bf16[1536,8,64]{0,2,1:T(8,128)(2,1)S(1)} %bitcast.64), kind=kOutput, calls=%fused_computation.11 | convolution fusion | flops 204471296 | bytes 8196096 | tf_op jit(solution)/shard_map/ihd,jhd->hij/dot_general | solution.py:33
  82.1 0.7 copy.25
  82.9 4.3 %fusion.7 = f32[8,128]{1,0:T(8,128)S(1)} fusion(f32[8,128,1536]{2,1,0:T(8,128)} %get-tuple-element.214, f32[8,128]{1,0:T(8,128)S(1)} %broadcast_maximum_fusion, pred[128,1536]{1,0:T(8,128)(4,1)S(1)} %broadcast_compare_fusion), kind=kLoop, calls=%fused_computation.12 | loop fusion | flops 4717568 | bytes 6496256 | tf_op jit(solution)/shard_map/reduce_sum | solution.py:37
  87.1 0.3 copy-done.2
  87.5 1.4 fusion.15
  88.8 0.8 copy-done.6
  89.6 2.1 fusion.31
  91.8 0.6 copy-done.9
  92.4 56.4 %all-gather.12.cloned.1.call-done = f32[512,4096]{1,0:T(8,128)} async-done(((f32[128,4096]{1,0:T(8,128)}), f32[512,4096]{1,0:T(8,128)}) %all-gather.12.cloned.1.call-update) | async-done | bytes 8388624 | tf_op jit(solution)/shard_map/all_gather | solution.py:98
  148.9 4.3 %reduce_sum.92 = f32[128,4096]{1,0:T(8,128)S(1)} reduce(f32[4,128,4096]{2,1,0:T(8,128)} %bitcast.63, f32[]{:T(128)} %constant.75.clone.1), dimensions={0}, to_apply=%region_3.4 | reduce | flops 1572864 | bytes 10485764 | tf_op jit(solution)/shard_map/reduce_sum | solution.py:97
  153.2 0.4 multiply_reduce_fusion
  153.6 0.3 fusion.12
  153.9 0.4 copy-done.7
  154.3 13.7 %fusion.30 = (f32[128]{0:T(128)S(1)}, f32[128,4096]{1,0:T(8,128)S(1)}) fusion(bf16[4096,4096]{1,0:T(8,128)(2,1)} %param.18, f32[128,4096]{1,0:T(8,128)S(1)} %fusion.12, f32[4096]{0:T(1024)S(1)} %copy-done.7), kind=kOutput, calls=%fused_computation.66 | convolution fusion | flops 4296540160 | bytes 37765632 | tf_op jit(solution)/shard_map/dot_general | solution.py:103
  168.1 0.7 select_reduce_fusion.1
  168.8 5.0 %all-gather.6 = f32[4,1,128]{2,1,0:T(1,128)S(1)} all-gather(f32[1,1,128]{2,1,0:T(1,128)S(1)} %bitcast.74), channel_id=5, replica_groups=mesh['dp'=8,'fsdp'=4] {'fsdp'}, dimensions={0}, use_global_device_ids=true | all-gather | bytes 2560 | tf_op jit(solution)/shard_map/all_gather | solution.py:10
  173.8 5.0 %all-gather.5 = f32[4,1,128]{2,1,0:T(1,128)S(1)} all-gather(f32[1,1,128]{2,1,0:T(1,128)S(1)} %bitcast.73), channel_id=4, replica_groups=mesh['dp'=8,'fsdp'=4] {'fsdp'}, dimensions={0}, use_global_device_ids=true | all-gather | bytes 2560 | tf_op jit(solution)/shard_map/all_gather | solution.py:10
  178.8 5.2 %all-gather.4 = f32[4,1,128]{2,1,0:T(1,128)S(1)} all-gather(f32[1,1,128]{2,1,0:T(1,128)S(1)} %bitcast.71), channel_id=3, replica_groups=mesh['dp'=8,'fsdp'=4] {'fsdp'}, dimensions={0}, use_global_device_ids=true | all-gather | bytes 2560 | tf_op jit(solution)/shard_map/all_gather | solution.py:10
  184.2 0.6 convert_reduce_fusion
  184.8 17.3 %convolution_bitcast_fusion = f32[4096,128]{0,1:T(8,128)} fusion(bf16[4096,4096]{1,0:T(8,128)(2,1)} %param.18, f32[128,4096]{1,0:T(8,128)S(1)} %get-tuple-element.216, f32[128]{0:T(128)S(1)} %get-tuple-element.209, f32[128]{0:T(128)S(1)} %convert_element_type.30, s32[128]{0:T(128)S(1)} %broadcast_subtract_fusion), kind=kOutput, calls=%fused_computation.14 | convolution fusion | flops 4298113024 | bytes 37750272 | tf_op jit(solution)/shard_map/dot_general | solution.py:119
  202.1 31.6 %reduce-scatter.2.cloned.1.call-done = f32[1024,128]{0,1:T(8,128)} async-done(((f32[4096,128]{0,1:T(8,128)}), f32[1024,128]{0,1:T(8,128)}) %reduce-scatter.2.cloned.1.call-update) | async-done | bytes 524304 | tf_op jit(solution)/shard_map/reduce_scatter | solution.py:118
  233.7 1.2 fusion.21
  234.9 5.8 %psum.30 = f32[128]{0:T(128)S(1)} all-reduce(f32[128]{0:T(128)S(1)} %get-tuple-element.185), channel_id=1, replica_groups=mesh['dp'=8,'fsdp'=4] {'fsdp'}, use_global_device_ids=true, to_apply=%region_16.17 | all-reduce | flops 128 | bytes 1024 | tf_op jit(solution)/shard_map/psum | solution.py:127
  240.7 22.5 %all-reduce = (f32[]{:T(128)}, f32[]{:T(128)}, f32[1024]{0:T(1024)S(1)}) all-reduce(f32[]{:T(128)} %get-tuple-element.189, f32[]{:T(128)} %get-tuple-element.188, f32[1024]{0:T(1024)S(1)} %get-tuple-element.184), channel_id=1, replica_groups=mesh['dp'=8,'fsdp'=4] {'dp'}, use_global_device_ids=true, to_apply=%region_11.12 | all-reduce | flops 1026 | bytes 8208 | tf_op jit(solution)/shard_map/psum | solution.py:130
  263.2 1.3 broadcast_divide_fusion
  265.9 2.6 divide_convert_fusion
  (42 shorter events, 0.8 us)
Async XLA Ops:
  7.2 4.2 %copy-start = (s32[8,4]{0,1:T(4,128)S(1)}, s32[8,4]{0,1:T(4,128)}, u32[]{:S(2)}) copy-start(s32[8,4]{0,1:T(4,128)} %param.21) | copy-start | bytes 388
  7.2 66.2 %all-gather.10.cloned.1.call-start = ((), (), s32[]{:S(2)}) async-start(), calls=%async_computation.1 | async-start | bytes 3538944 | tf_op jit(solution)/shard_map/all_gather | solution.py:83
  7.9 140.9 %all-gather.12.cloned.1.call-start = ((), (), s32[]{:S(2)}) async-start(), calls=%async_computation.3 | async-start | bytes 10485760 | tf_op jit(solution)/shard_map/all_gather | solution.py:98
  8.0 3.6 %copy-start.10 = (s32[128]{0:T(128)S(1)}, s32[128]{0:T(128)}, u32[]{:S(2)}) copy-start(s32[128]{0:T(128)} %param.20) | copy-start | bytes 1540
  8.0 3.7 %copy-start.8 = (s32[1536]{0:T(1024)S(1)}, s32[1536]{0:T(1024)}, u32[]{:S(2)}) copy-start(s32[1536]{0:T(1024)} %param.19) | copy-start | bytes 18436
  82.8 4.6 %copy-start.2 = (f32[8,128,1536]{2,1,0:T(8,128)S(1)}, f32[8,128,1536]{2,1,0:T(8,128)}, u32[]{:S(2)}) copy-start(f32[8,128,1536]{2,1,0:T(8,128)} %get-tuple-element.214) | copy-start | bytes 18874372
  87.4 2.2 copy-start.6
  91.8 0.7 copy-start.9
  91.8 0.7 copy-start.11
  91.8 141.9 %reduce-scatter.2.cloned.1.call-start = ((), (), s32[]{:S(2)}) async-start(), calls=%async_computation.2 | async-start | bytes 2621440 | tf_op jit(solution)/shard_map/reduce_scatter | solution.py:118
  148.9 4.3 %copy-start.5 = (bf16[128,4096]{1,0:T(8,128)(2,1)S(1)}, bf16[128,4096]{1,0:T(8,128)(2,1)}, u32[]{:S(2)}) copy-start(bf16[128,4096]{1,0:T(8,128)(2,1)} %param.13) | copy-start | bytes 3145732
  153.6 0.7 copy-start.7
  154.3 13.8 %copy-start.3 = (f32[128,4096]{1,0:T(8,128)}, f32[128,4096]{1,0:T(8,128)S(1)}, u32[]{:S(2)}) copy-start(f32[128,4096]{1,0:T(8,128)S(1)} %fusion.12) | copy-start | bytes 6291460
  202.1 31.6 %copy-start.4 = (f32[128,4096]{1,0:T(8,128)S(1)}, f32[128,4096]{1,0:T(8,128)}, u32[]{:S(2)}) copy-start(f32[128,4096]{1,0:T(8,128)} %copy-done.3) | copy-start | bytes 6291460
  202.1 66.4 %copy-start.1 = (s32[8,4]{0,1:T(4,128)S(1)}, s32[8,4]{0,1:T(4,128)}, u32[]{:S(2)}) copy-start(s32[8,4]{0,1:T(4,128)} %param.21) | copy-start | bytes 388
Sparse Core Ops, SparseCore 0:
  10.2 63.1 all-gather.9
  91.9 56.8 all-gather.11
  202.2 31.4 reduce-scatter.1
